TPU v7x, 512 devices: a whole 4x8x8 slice. The times are simulated.
512 devices in a mesh: section: 16 (over x_hi, y), dp: 8 (over z), mp: 4 (over x_lo, core).
Axes of the slice: x: 4 (x_hi: 2, x_lo: 2; x = x_hi * 2 + x_lo), y: 8, z: 8, core: 2. Of those that a mesh axis runs over, the one named last changes fastest.
Arguments:
- cotangent: bfloat16 [1024, 4096], P('dp', 'mp'), may hold values from -6 to 6
- saved_inputs: bfloat16 [16, 1024, 4096], P('section', 'dp', 'mp'), may hold values from -6 to 6
- pre_acts: bfloat16 [16, 1024, 4096], P('section', 'dp', 'mp'), may hold values from -8 to 8
- weights: bfloat16 [16, 4096, 4096], P('section', 'mp', 'dp'), may hold values from -0.046875 to 0.046875
- proj_in: bfloat16 [16, 4096, 64], P('section', 'mp'), may hold values from -0.09375 to 0.09375
- proj_out: bfloat16 [16, 4096, 64], P('section', 'mp'), may hold values from -0.09375 to 0.09375
- query_panels: float32 [16, 16, 4096], P('section', 'dp', 'mp'), may hold values from -4 to 4
- partners: int32 [8, 8], replicated, may hold values from 0 to 7, as said below
Outputs:
- train_panels: float32 [16, 32, 4096], P('section', 'dp', 'mp')
- scores: float32 [16, 8, 4], replicated
Inputs may be any that keep to these rules, and one draw needn't show every extreme that they name: The plan has 8 rounds: one round pairs every dp index with itself, and the others are the rounds of one round-robin plan of the 8 indices. The rows of partners hold each of these rounds once, in some order, so partners[r, partners[r, i]] = i.
All inputs are finite; a program needn't handle non-finite values.
Results may differ from a plain program's by a relative error of at most 0.02.
Values may be sent and summed in bfloat16 or wider, within the bound.
No kernel may reach another device: no remote copies, remote signals or barrier semaphores. Data moves between devices by JAX's collectives and lax.ppermute only.
A program may use at most 64 MiB of HBM per device.

v0:
```python
import math
import jax
import jax.numpy as jnp
from jax import lax
from jax.sharding import PartitionSpec as P

LEN = 32


def from_behind(block, axis, distance):
    devices = range(lax.axis_size(axis))
    route = [(i - distance, i) for i in devices if i - distance in devices]
    return lax.ppermute(block, axis, route)


def silu_slope(pre_state):
    sigma = jax.nn.sigmoid(pre_state)
    return sigma * (1.0 + pre_state * (1.0 - sigma))


def score_pair(query_rows, train_rows):
    return jnp.dot(query_rows, train_rows.T, precision=lax.Precision.HIGHEST)


def place_block(score_table, block, row_at, col_at):
    return lax.dynamic_update_slice(
        score_table,
        block[None, None],
        (jnp.asarray(row_at, jnp.int32), jnp.int32(col_at), jnp.int32(0), jnp.int32(0)),
    )


def body(cotangent, saved_inputs, pre_acts, weights, proj_in, proj_out, query_panels, partners):
    section_count = lax.axis_size("section")
    model_count = lax.axis_size("mp")
    data_count = lax.axis_size("dp")
    section_index = lax.axis_index("section")
    model_index = lax.axis_index("mp")
    data_index = lax.axis_index("dp")
    inputs = saved_inputs[0]
    pre_state = pre_acts[0]
    columns = inputs.shape[1]
    length = LEN
    examples = inputs.shape[0] // length
    low_rank = proj_in.shape[2]
    w_rows = lax.all_gather(weights[0], "dp", axis=1, tiled=True)
    step_count = examples + section_count - 1
    top_section = section_count - 1

    def advance(turn, carry):
        outgoing, stored, side_store = carry
        received = from_behind(outgoing, "section", -1)
        example_at = turn - (top_section - section_index)
        active = jnp.logical_and(example_at >= 0, example_at < examples)
        row_start = jnp.clip(example_at, 0, examples - 1) * length
        top_grad = lax.dynamic_slice_in_dim(cotangent, row_start, length, 0)
        delta_piece = jnp.where(section_index == top_section, top_grad, received)
        slopes = silu_slope(
            lax.dynamic_slice_in_dim(pre_state, row_start, length, 0).astype(jnp.float32)
        )
        grad_piece = (delta_piece.astype(jnp.float32) * slopes).astype(jnp.bfloat16)
        grad_full = lax.all_gather(grad_piece, "mp", axis=1, tiled=True)

        def through():
            back_term = lax.dot_general(
                grad_full, w_rows, (((1,), (1,)), ((), ())), preferred_element_type=jnp.float32
            )
            return (delta_piece.astype(jnp.float32) + back_term).astype(jnp.bfloat16)

        def skipped():
            return jnp.zeros_like(delta_piece)

        passed = lax.cond(active, through, skipped)
        previous = lax.dynamic_slice_in_dim(stored, row_start, length, 0)
        stored = lax.dynamic_update_slice_in_dim(
            stored, jnp.where(active, grad_piece, previous), row_start, 0
        )
        return (passed, stored, side_store)

    initial = (
        jnp.zeros((length, columns), jnp.bfloat16),
        jnp.zeros((inputs.shape[0], columns), jnp.bfloat16),
        jnp.zeros((inputs.shape[0], low_rank), jnp.float32),
    )
    final_state = lax.fori_loop(0, step_count, advance, initial)
    stored = final_state[1]
    side_store = final_state[2]
    in_part = jnp.dot(inputs, proj_in[0], preferred_element_type=jnp.float32)
    out_part = jnp.dot(stored, proj_out[0], preferred_element_type=jnp.float32)
    in_side, out_side = (
        lax.psum(in_part.astype(jnp.bfloat16), "mp").astype(jnp.float32),
        lax.psum(out_part.astype(jnp.bfloat16), "mp").astype(jnp.float32),
    )
    piece_rank = low_rank // model_count
    in_rows = lax.dynamic_slice_in_dim(in_side, model_index * piece_rank, piece_rank, 1)
    panels_here = jnp.einsum(
        "etr,etc->erc",
        in_rows.reshape(examples, length, piece_rank),
        out_side.reshape(examples, length, low_rank),
        precision=lax.Precision.HIGHEST,
    ) / math.sqrt(length)
    panels_here = panels_here.reshape(examples, piece_rank * low_rank)
    queries = query_panels[0]
    asked = queries.shape[0]
    rounds = partners.shape[0]
    score_scale = 1.0 / (low_rank * math.sqrt(section_count))
    score_table = jnp.zeros((data_count, rounds, asked, examples), jnp.float32)
    everyone = lax.all_gather(panels_here, "dp", axis=0, tiled=True).reshape(
        data_count, examples, -1
    )
    for round_at in range(rounds):
        partner = partners[round_at, data_index]
        chosen = lax.dynamic_index_in_dim(everyone, partner, 0, keepdims=False)
        score_table = place_block(score_table, score_pair(queries, chosen), data_index, round_at)
    summed = lax.psum(score_table * score_scale, ("section", "dp", "mp"))
    scores = summed.transpose(0, 2, 1, 3).reshape(data_count * asked, rounds, examples)
    return (panels_here[None], scores)


def solution(mesh):
    placed = (
        P("dp", "mp"),
        P("section", "dp", "mp"),
        P("section", "dp", "mp"),
        P("section", "mp", "dp"),
        P("section", "mp", None),
        P("section", "mp", None),
        P("section", "dp", "mp"),
        P(),
    )
    return jax.shard_map(
        body, mesh=mesh, in_specs=placed, out_specs=(P("section", "dp", "mp"), P()), check_vma=False
    )
```

profile of v0, /device:TPU:1, one launch (start us, length us, event | category | flops | bytes accessed | tf_op | source)
XLA Modules:
  0.0 635.7 jit_solution(11931362347134518088)
XLA Ops:
  25.3 87.9 %all-gather.4.cloned.1.call-done = bf16[1,1024,4096]{2,1,0:T(8,128)(2,1)} async-done(((bf16[1,1024,512]{2,1,0:T(8,128)(2,1)}), bf16[1,1024,4096]{2,1,0:T(8,128)(2,1)}) %all-gather.4.cloned.1.call-update) | async-done | bytes 8388624 | tf_op jit(solution)/shard_map/all_gather | solution.py:46
  113.8 380.4 %while.17 = (s32[]{:T(128)}, bf16[32,1024]{1,0:T(8,128)(2,1)}, bf16[128,1024]{1,0:T(8,128)(2,1)S(1)}, s32[]{:T(128)}, pred[]{:T(512)}, /*index=5*/bf16[128,1024]...) while((s32[]{:T(128)}, bf16[32,1024]{1,0:T(8,128)(2,1)}, ...), condition=%wide.region_4.5_spmd, body=%wide.region_1.4_spmd.sunk | while | flops 268959744 | bytes 9830719 | solution.py:85
  120.2 7.4 %all_gather.18 = bf16[32,4096]{1,0:T(8,128)(2,1)S(1)} all-gather(bf16[32,1024]{1,0:T(8,128)(2,1)S(1)} %get-tuple-element.282), channel_id=1, replica_groups=mesh['section'=16,'dp'=8,'mp'=4] {'mp'}, dimensions={1}, use_global_device_ids=true | all-gather | bytes 327680 | tf_op jit(solution)/shard_map/while/body/eval_jaxpr/all_gather | solution.py:62
  134.8 6.6 %all_gather.18 = bf16[32,4096]{1,0:T(8,128)(2,1)S(1)} all-gather(bf16[32,1024]{1,0:T(8,128)(2,1)S(1)} %get-tuple-element.282), channel_id=1, replica_groups=mesh['section'=16,'dp'=8,'mp'=4] {'mp'}, dimensions={1}, use_global_device_ids=true | all-gather | bytes 327680 | tf_op jit(solution)/shard_map/while/body/eval_jaxpr/all_gather | solution.py:62
  148.7 6.6 %all_gather.18 = bf16[32,4096]{1,0:T(8,128)(2,1)S(1)} all-gather(bf16[32,1024]{1,0:T(8,128)(2,1)S(1)} %get-tuple-element.282), channel_id=1, replica_groups=mesh['section'=16,'dp'=8,'mp'=4] {'mp'}, dimensions={1}, use_global_device_ids=true | all-gather | bytes 327680 | tf_op jit(solution)/shard_map/while/body/eval_jaxpr/all_gather | solution.py:62
  163.2 6.4 %all_gather.18 = bf16[32,4096]{1,0:T(8,128)(2,1)S(1)} all-gather(bf16[32,1024]{1,0:T(8,128)(2,1)S(1)} %get-tuple-element.282), channel_id=1, replica_groups=mesh['section'=16,'dp'=8,'mp'=4] {'mp'}, dimensions={1}, use_global_device_ids=true | all-gather | bytes 327680 | tf_op jit(solution)/shard_map/while/body/eval_jaxpr/all_gather | solution.py:62
  193.2 6.4 %all_gather.18 = bf16[32,4096]{1,0:T(8,128)(2,1)S(1)} all-gather(bf16[32,1024]{1,0:T(8,128)(2,1)S(1)} %get-tuple-element.282), channel_id=1, replica_groups=mesh['section'=16,'dp'=8,'mp'=4] {'mp'}, dimensions={1}, use_global_device_ids=true | all-gather | bytes 327680 | tf_op jit(solution)/shard_map/while/body/eval_jaxpr/all_gather | solution.py:62
  208.2 6.4 %all_gather.18 = bf16[32,4096]{1,0:T(8,128)(2,1)S(1)} all-gather(bf16[32,1024]{1,0:T(8,128)(2,1)S(1)} %get-tuple-element.282), channel_id=1, replica_groups=mesh['section'=16,'dp'=8,'mp'=4] {'mp'}, dimensions={1}, use_global_device_ids=true | all-gather | bytes 327680 | tf_op jit(solution)/shard_map/while/body/eval_jaxpr/all_gather | solution.py:62
  223.2 6.4 %all_gather.18 = bf16[32,4096]{1,0:T(8,128)(2,1)S(1)} all-gather(bf16[32,1024]{1,0:T(8,128)(2,1)S(1)} %get-tuple-element.282), channel_id=1, replica_groups=mesh['section'=16,'dp'=8,'mp'=4] {'mp'}, dimensions={1}, use_global_device_ids=true | all-gather | bytes 327680 | tf_op jit(solution)/shard_map/while/body/eval_jaxpr/all_gather | solution.py:62
  238.3 6.4 %all_gather.18 = bf16[32,4096]{1,0:T(8,128)(2,1)S(1)} all-gather(bf16[32,1024]{1,0:T(8,128)(2,1)S(1)} %get-tuple-element.282), channel_id=1, replica_groups=mesh['section'=16,'dp'=8,'mp'=4] {'mp'}, dimensions={1}, use_global_device_ids=true | all-gather | bytes 327680 | tf_op jit(solution)/shard_map/while/body/eval_jaxpr/all_gather | solution.py:62
  253.3 6.4 %all_gather.18 = bf16[32,4096]{1,0:T(8,128)(2,1)S(1)} all-gather(bf16[32,1024]{1,0:T(8,128)(2,1)S(1)} %get-tuple-element.282), channel_id=1, replica_groups=mesh['section'=16,'dp'=8,'mp'=4] {'mp'}, dimensions={1}, use_global_device_ids=true | all-gather | bytes 327680 | tf_op jit(solution)/shard_map/while/body/eval_jaxpr/all_gather | solution.py:62
  261.6 8.1 %collective-permute-done = bf16[32,1024]{1,0:T(8,128)(2,1)S(1)} collective-permute-done((bf16[32,1024]{1,0:T(8,128)(2,1)}, bf16[32,1024]{1,0:T(8,128)(2,1)S(1)}, u32[]{:S(2)}, u32[]{:S(2)}) %collective-permute-start) | collective-permute-done | bytes 65568 | tf_op jit(solution)/shard_map/while/body/eval_jaxpr/ppermute | solution.py:13
  270.6 6.4 %all_gather.18 = bf16[32,4096]{1,0:T(8,128)(2,1)S(1)} all-gather(bf16[32,1024]{1,0:T(8,128)(2,1)S(1)} %get-tuple-element.282), channel_id=1, replica_groups=mesh['section'=16,'dp'=8,'mp'=4] {'mp'}, dimensions={1}, use_global_device_ids=true | all-gather | bytes 327680 | tf_op jit(solution)/shard_map/while/body/eval_jaxpr/all_gather | solution.py:62
  278.9 8.2 %collective-permute-done = bf16[32,1024]{1,0:T(8,128)(2,1)S(1)} collective-permute-done((bf16[32,1024]{1,0:T(8,128)(2,1)}, bf16[32,1024]{1,0:T(8,128)(2,1)S(1)}, u32[]{:S(2)}, u32[]{:S(2)}) %collective-permute-start) | collective-permute-done | bytes 65568 | tf_op jit(solution)/shard_map/while/body/eval_jaxpr/ppermute | solution.py:13
  296.3 8.2 %collective-permute-done = bf16[32,1024]{1,0:T(8,128)(2,1)S(1)} collective-permute-done((bf16[32,1024]{1,0:T(8,128)(2,1)}, bf16[32,1024]{1,0:T(8,128)(2,1)S(1)}, u32[]{:S(2)}, u32[]{:S(2)}) %collective-permute-start) | collective-permute-done | bytes 65568 | tf_op jit(solution)/shard_map/while/body/eval_jaxpr/ppermute | solution.py:13
  313.8 8.2 %collective-permute-done = bf16[32,1024]{1,0:T(8,128)(2,1)S(1)} collective-permute-done((bf16[32,1024]{1,0:T(8,128)(2,1)}, bf16[32,1024]{1,0:T(8,128)(2,1)S(1)}, u32[]{:S(2)}, u32[]{:S(2)}) %collective-permute-start) | collective-permute-done | bytes 65568 | tf_op jit(solution)/shard_map/while/body/eval_jaxpr/ppermute | solution.py:13
  331.2 8.2 %collective-permute-done = bf16[32,1024]{1,0:T(8,128)(2,1)S(1)} collective-permute-done((bf16[32,1024]{1,0:T(8,128)(2,1)}, bf16[32,1024]{1,0:T(8,128)(2,1)S(1)}, u32[]{:S(2)}, u32[]{:S(2)}) %collective-permute-start) | collective-permute-done | bytes 65568 | tf_op jit(solution)/shard_map/while/body/eval_jaxpr/ppermute | solution.py:13
  348.6 61.6 %collective-permute-done = bf16[32,1024]{1,0:T(8,128)(2,1)S(1)} collective-permute-done((bf16[32,1024]{1,0:T(8,128)(2,1)}, bf16[32,1024]{1,0:T(8,128)(2,1)S(1)}, u32[]{:S(2)}, u32[]{:S(2)}) %collective-permute-start) | collective-permute-done | bytes 65568 | tf_op jit(solution)/shard_map/while/body/eval_jaxpr/ppermute | solution.py:13
  417.5 6.6 %conditional.2 = (bf16[32,1024]{1,0:T(8,128)(2,1)}) conditional(s32[]{:T(128)} %convert_element_type.80, () %tuple.60, (bf16[32,1024]{1,0:T(8,128)(2,1)S(1)}, bf16[32,4096]{1,0:T(8,128)(2,1)S(1)}, bf16[1024,4096]{1,0:T(8,128)(2,1)}) %tuple.61), branch_computations={%region_2.2_spmd, %region_3.3_spmd} | conditional | flops 268533760 | bytes 8781832 | solution.py:73
  417.5 6.6 %fusion = bf16[32,1024]{1,0:T(8,128)(2,1)} fusion(bf16[32,4096]{1,0:T(8,128)(2,1)S(1)} %get-tuple-element.181, bf16[1024,4096]{1,0:T(8,128)(2,1)} %get-tuple-element.182, bf16[32,1024]{1,0:T(8,128)(2,1)S(1)} %get-tuple-element.180), kind=kOutput, calls=%fused_computation.1 | convolution fusion | flops 268533760 | bytes 8781824 | tf_op jit(solution)/shard_map/while/body/eval_jaxpr/cond/branch_1_fun/dot_general | solution.py:65
  425.4 8.2 %collective-permute-done = bf16[32,1024]{1,0:T(8,128)(2,1)S(1)} collective-permute-done((bf16[32,1024]{1,0:T(8,128)(2,1)}, bf16[32,1024]{1,0:T(8,128)(2,1)S(1)}, u32[]{:S(2)}, u32[]{:S(2)}) %collective-permute-start) | collective-permute-done | bytes 65568 | tf_op jit(solution)/shard_map/while/body/eval_jaxpr/ppermute | solution.py:13
  440.8 6.6 %conditional.2 = (bf16[32,1024]{1,0:T(8,128)(2,1)}) conditional(s32[]{:T(128)} %convert_element_type.80, () %tuple.60, (bf16[32,1024]{1,0:T(8,128)(2,1)S(1)}, bf16[32,4096]{1,0:T(8,128)(2,1)S(1)}, bf16[1024,4096]{1,0:T(8,128)(2,1)}) %tuple.61), branch_computations={%region_2.2_spmd, %region_3.3_spmd} | conditional | flops 268533760 | bytes 8781832 | solution.py:73
  440.8 6.6 %fusion = bf16[32,1024]{1,0:T(8,128)(2,1)} fusion(bf16[32,4096]{1,0:T(8,128)(2,1)S(1)} %get-tuple-element.181, bf16[1024,4096]{1,0:T(8,128)(2,1)} %get-tuple-element.182, bf16[32,1024]{1,0:T(8,128)(2,1)S(1)} %get-tuple-element.180), kind=kOutput, calls=%fused_computation.1 | convolution fusion | flops 268533760 | bytes 8781824 | tf_op jit(solution)/shard_map/while/body/eval_jaxpr/cond/branch_1_fun/dot_general | solution.py:65
  448.7 8.3 %collective-permute-done = bf16[32,1024]{1,0:T(8,128)(2,1)S(1)} collective-permute-done((bf16[32,1024]{1,0:T(8,128)(2,1)}, bf16[32,1024]{1,0:T(8,128)(2,1)S(1)}, u32[]{:S(2)}, u32[]{:S(2)}) %collective-permute-start) | collective-permute-done | bytes 65568 | tf_op jit(solution)/shard_map/while/body/eval_jaxpr/ppermute | solution.py:13
  464.3 6.6 %conditional.2 = (bf16[32,1024]{1,0:T(8,128)(2,1)}) conditional(s32[]{:T(128)} %convert_element_type.80, () %tuple.60, (bf16[32,1024]{1,0:T(8,128)(2,1)S(1)}, bf16[32,4096]{1,0:T(8,128)(2,1)S(1)}, bf16[1024,4096]{1,0:T(8,128)(2,1)}) %tuple.61), branch_computations={%region_2.2_spmd, %region_3.3_spmd} | conditional | flops 268533760 | bytes 8781832 | solution.py:73
  464.3 6.6 %fusion = bf16[32,1024]{1,0:T(8,128)(2,1)} fusion(bf16[32,4096]{1,0:T(8,128)(2,1)S(1)} %get-tuple-element.181, bf16[1024,4096]{1,0:T(8,128)(2,1)} %get-tuple-element.182, bf16[32,1024]{1,0:T(8,128)(2,1)S(1)} %get-tuple-element.180), kind=kOutput, calls=%fused_computation.1 | convolution fusion | flops 268533760 | bytes 8781824 | tf_op jit(solution)/shard_map/while/body/eval_jaxpr/cond/branch_1_fun/dot_general | solution.py:65
  472.2 8.2 %collective-permute-done = bf16[32,1024]{1,0:T(8,128)(2,1)S(1)} collective-permute-done((bf16[32,1024]{1,0:T(8,128)(2,1)}, bf16[32,1024]{1,0:T(8,128)(2,1)S(1)}, u32[]{:S(2)}, u32[]{:S(2)}) %collective-permute-start) | collective-permute-done | bytes 65568 | tf_op jit(solution)/shard_map/while/body/eval_jaxpr/ppermute | solution.py:13
  487.7 6.6 %conditional.2 = (bf16[32,1024]{1,0:T(8,128)(2,1)}) conditional(s32[]{:T(128)} %convert_element_type.80, () %tuple.60, (bf16[32,1024]{1,0:T(8,128)(2,1)S(1)}, bf16[32,4096]{1,0:T(8,128)(2,1)S(1)}, bf16[1024,4096]{1,0:T(8,128)(2,1)}) %tuple.61), branch_computations={%region_2.2_spmd, %region_3.3_spmd} | conditional | flops 268533760 | bytes 8781832 | solution.py:73
  487.7 6.6 %fusion = bf16[32,1024]{1,0:T(8,128)(2,1)} fusion(bf16[32,4096]{1,0:T(8,128)(2,1)S(1)} %get-tuple-element.181, bf16[1024,4096]{1,0:T(8,128)(2,1)} %get-tuple-element.182, bf16[32,1024]{1,0:T(8,128)(2,1)S(1)} %get-tuple-element.180), kind=kOutput, calls=%fused_computation.1 | convolution fusion | flops 268533760 | bytes 8781824 | tf_op jit(solution)/shard_map/while/body/eval_jaxpr/cond/branch_1_fun/dot_general | solution.py:65
  494.6 10.8 %all-reduce = (bf16[4,32,64]{2,1,0:T(8,128)(2,1)S(1)}, bf16[128,64]{0,1:T(8,128)(2,1)S(1)}) all-reduce(bf16[4,32,64]{2,1,0:T(8,128)(2,1)S(1)} %bitcast.104, bf16[128,64]{0,1:T(8,128)(2,1)S(1)} %convolution_convert_fusion.1), channel_id=1, replica_groups=mesh['section'=16,'dp'=8,'mp'=4] {'mp'}, use_global_device_ids=true, to_apply=%region_5.6 | all-reduce | flops 16384 | bytes 65536 | tf_op jit(solution)/shard_map/psum | solution.py:92
  505.7 18.5 %all-gather.1 = f32[8,4,1024]{2,1,0:T(4,128)S(1)} all-gather(f32[1,4,1024]{2,1,0:T(4,128)S(1)} %broadcast_in_dim_reshape.3), channel_id=1, replica_groups=mesh['section'=16,'dp'=8,'mp'=4] {'dp'}, dimensions={0}, use_global_device_ids=true | all-gather | bytes 147456 | tf_op jit(solution)/shard_map/all_gather | solution.py:108
  529.0 99.2 %psum.23 = f32[16,8,4]{1,0,2:T(8,128)S(1)} all-reduce(f32[16,8,4]{1,0,2:T(8,128)S(1)} %bitcast.105), channel_id=1, replica_groups=mesh['section'=16,'dp'=8,'mp'=4] {'section','dp','mp'}, use_global_device_ids=true, to_apply=%region_6.7 | all-reduce | flops 512 | bytes 4096 | tf_op jit(solution)/shard_map/psum | solution.py:115
  (134 shorter events, 180.7 us)
Async XLA Ops:
  7.2 17.0 %copy-start = (bf16[1,128,1024]{2,1,0:T(8,128)(2,1)S(1)}, bf16[1,128,1024]{2,1,0:T(8,128)(2,1)}, u32[]{:S(2)}) copy-start(bf16[1,128,1024]{2,1,0:T(8,128)(2,1)} %param.13) | copy-start | bytes 786436
  7.2 106.0 %all-gather.4.cloned.1.call-start = ((), (), s32[]{:S(2)}) async-start(), calls=%async_computation | async-start | bytes 9437184 | tf_op jit(solution)/shard_map/all_gather | solution.py:46
  113.8 380.5 %copy-start.2 = (bf16[1,1024,64]{1,2,0:T(8,128)(2,1)S(1)}, bf16[1,1024,64]{1,2,0:T(8,128)(2,1)}, u32[]{:S(2)}) copy-start(bf16[1,1024,64]{1,2,0:T(8,128)(2,1)} %param.17) | copy-start | bytes 393220
  113.8 410.4 %copy-start.1 = (f32[1,2,1024]{2,1,0:T(2,128)S(1)}, f32[1,2,1024]{2,1,0:T(2,128)}, u32[]{:S(2)}) copy-start(f32[1,2,1024]{2,1,0:T(2,128)} %param.18) | copy-start | bytes 24580
  113.9 5.4 collective-permute-start
  128.2 5.6 collective-permute-start
  142.1 5.6 collective-permute-start
  155.9 6.3 collective-permute-start
  170.1 7.1 %collective-permute-start = (bf16[32,1024]{1,0:T(8,128)(2,1)}, bf16[32,1024]{1,0:T(8,128)(2,1)S(1)}, u32[]{:S(2)}, u32[]{:S(2)}) collective-permute-start(bf16[32,1024]{1,0:T(8,128)(2,1)} %get-tuple-element.299), channel_id=1, source_target_pairs={{32,0},{64,32},{96,64},{128,96},{160,128},{192,160},{224,192},{256... | collective-permute-start | bytes 196616 | tf_op jit(solution)/shard_map/while/body/eval_jaxpr/ppermute | solution.py:13
  185.2 7.1 %collective-permute-start = (bf16[32,1024]{1,0:T(8,128)(2,1)}, bf16[32,1024]{1,0:T(8,128)(2,1)S(1)}, u32[]{:S(2)}, u32[]{:S(2)}) collective-permute-start(bf16[32,1024]{1,0:T(8,128)(2,1)} %get-tuple-element.299), channel_id=1, source_target_pairs={{32,0},{64,32},{96,64},{128,96},{160,128},{192,160},{224,192},{256... | collective-permute-start | bytes 196616 | tf_op jit(solution)/shard_map/while/body/eval_jaxpr/ppermute | solution.py:13
  200.2 7.1 %collective-permute-start = (bf16[32,1024]{1,0:T(8,128)(2,1)}, bf16[32,1024]{1,0:T(8,128)(2,1)S(1)}, u32[]{:S(2)}, u32[]{:S(2)}) collective-permute-start(bf16[32,1024]{1,0:T(8,128)(2,1)} %get-tuple-element.299), channel_id=1, source_target_pairs={{32,0},{64,32},{96,64},{128,96},{160,128},{192,160},{224,192},{256... | collective-permute-start | bytes 196616 | tf_op jit(solution)/shard_map/while/body/eval_jaxpr/ppermute | solution.py:13
  215.2 7.1 %collective-permute-start = (bf16[32,1024]{1,0:T(8,128)(2,1)}, bf16[32,1024]{1,0:T(8,128)(2,1)S(1)}, u32[]{:S(2)}, u32[]{:S(2)}) collective-permute-start(bf16[32,1024]{1,0:T(8,128)(2,1)} %get-tuple-element.299), channel_id=1, source_target_pairs={{32,0},{64,32},{96,64},{128,96},{160,128},{192,160},{224,192},{256... | collective-permute-start | bytes 196616 | tf_op jit(solution)/shard_map/while/body/eval_jaxpr/ppermute | solution.py:13
  230.2 7.1 %collective-permute-start = (bf16[32,1024]{1,0:T(8,128)(2,1)}, bf16[32,1024]{1,0:T(8,128)(2,1)S(1)}, u32[]{:S(2)}, u32[]{:S(2)}) collective-permute-start(bf16[32,1024]{1,0:T(8,128)(2,1)} %get-tuple-element.299), channel_id=1, source_target_pairs={{32,0},{64,32},{96,64},{128,96},{160,128},{192,160},{224,192},{256... | collective-permute-start | bytes 196616 | tf_op jit(solution)/shard_map/while/body/eval_jaxpr/ppermute | solution.py:13
  245.3 7.1 %collective-permute-start = (bf16[32,1024]{1,0:T(8,128)(2,1)}, bf16[32,1024]{1,0:T(8,128)(2,1)S(1)}, u32[]{:S(2)}, u32[]{:S(2)}) collective-permute-start(bf16[32,1024]{1,0:T(8,128)(2,1)} %get-tuple-element.299), channel_id=1, source_target_pairs={{32,0},{64,32},{96,64},{128,96},{160,128},{192,160},{224,192},{256... | collective-permute-start | bytes 196616 | tf_op jit(solution)/shard_map/while/body/eval_jaxpr/ppermute | solution.py:13
  260.3 9.4 %collective-permute-start = (bf16[32,1024]{1,0:T(8,128)(2,1)}, bf16[32,1024]{1,0:T(8,128)(2,1)S(1)}, u32[]{:S(2)}, u32[]{:S(2)}) collective-permute-start(bf16[32,1024]{1,0:T(8,128)(2,1)} %get-tuple-element.299), channel_id=1, source_target_pairs={{32,0},{64,32},{96,64},{128,96},{160,128},{192,160},{224,192},{256... | collective-permute-start | bytes 196616 | tf_op jit(solution)/shard_map/while/body/eval_jaxpr/ppermute | solution.py:13
  277.6 9.5 %collective-permute-start = (bf16[32,1024]{1,0:T(8,128)(2,1)}, bf16[32,1024]{1,0:T(8,128)(2,1)S(1)}, u32[]{:S(2)}, u32[]{:S(2)}) collective-permute-start(bf16[32,1024]{1,0:T(8,128)(2,1)} %get-tuple-element.299), channel_id=1, source_target_pairs={{32,0},{64,32},{96,64},{128,96},{160,128},{192,160},{224,192},{256... | collective-permute-start | bytes 196616 | tf_op jit(solution)/shard_map/while/body/eval_jaxpr/ppermute | solution.py:13
  295.0 9.5 %collective-permute-start = (bf16[32,1024]{1,0:T(8,128)(2,1)}, bf16[32,1024]{1,0:T(8,128)(2,1)S(1)}, u32[]{:S(2)}, u32[]{:S(2)}) collective-permute-start(bf16[32,1024]{1,0:T(8,128)(2,1)} %get-tuple-element.299), channel_id=1, source_target_pairs={{32,0},{64,32},{96,64},{128,96},{160,128},{192,160},{224,192},{256... | collective-permute-start | bytes 196616 | tf_op jit(solution)/shard_map/while/body/eval_jaxpr/ppermute | solution.py:13
  312.4 9.5 %collective-permute-start = (bf16[32,1024]{1,0:T(8,128)(2,1)}, bf16[32,1024]{1,0:T(8,128)(2,1)S(1)}, u32[]{:S(2)}, u32[]{:S(2)}) collective-permute-start(bf16[32,1024]{1,0:T(8,128)(2,1)} %get-tuple-element.299), channel_id=1, source_target_pairs={{32,0},{64,32},{96,64},{128,96},{160,128},{192,160},{224,192},{256... | collective-permute-start | bytes 196616 | tf_op jit(solution)/shard_map/while/body/eval_jaxpr/ppermute | solution.py:13
  329.9 9.5 %collective-permute-start = (bf16[32,1024]{1,0:T(8,128)(2,1)}, bf16[32,1024]{1,0:T(8,128)(2,1)S(1)}, u32[]{:S(2)}, u32[]{:S(2)}) collective-permute-start(bf16[32,1024]{1,0:T(8,128)(2,1)} %get-tuple-element.299), channel_id=1, source_target_pairs={{32,0},{64,32},{96,64},{128,96},{160,128},{192,160},{224,192},{256... | collective-permute-start | bytes 196616 | tf_op jit(solution)/shard_map/while/body/eval_jaxpr/ppermute | solution.py:13
  347.3 62.9 %collective-permute-start = (bf16[32,1024]{1,0:T(8,128)(2,1)}, bf16[32,1024]{1,0:T(8,128)(2,1)S(1)}, u32[]{:S(2)}, u32[]{:S(2)}) collective-permute-start(bf16[32,1024]{1,0:T(8,128)(2,1)} %get-tuple-element.299), channel_id=1, source_target_pairs={{32,0},{64,32},{96,64},{128,96},{160,128},{192,160},{224,192},{256... | collective-permute-start | bytes 196616 | tf_op jit(solution)/shard_map/while/body/eval_jaxpr/ppermute | solution.py:13
  424.0 9.6 %collective-permute-start = (bf16[32,1024]{1,0:T(8,128)(2,1)}, bf16[32,1024]{1,0:T(8,128)(2,1)S(1)}, u32[]{:S(2)}, u32[]{:S(2)}) collective-permute-start(bf16[32,1024]{1,0:T(8,128)(2,1)} %get-tuple-element.299), channel_id=1, source_target_pairs={{32,0},{64,32},{96,64},{128,96},{160,128},{192,160},{224,192},{256... | collective-permute-start | bytes 196616 | tf_op jit(solution)/shard_map/while/body/eval_jaxpr/ppermute | solution.py:13
  447.4 9.6 %collective-permute-start = (bf16[32,1024]{1,0:T(8,128)(2,1)}, bf16[32,1024]{1,0:T(8,128)(2,1)S(1)}, u32[]{:S(2)}, u32[]{:S(2)}) collective-permute-start(bf16[32,1024]{1,0:T(8,128)(2,1)} %get-tuple-element.299), channel_id=1, source_target_pairs={{32,0},{64,32},{96,64},{128,96},{160,128},{192,160},{224,192},{256... | collective-permute-start | bytes 196616 | tf_op jit(solution)/shard_map/while/body/eval_jaxpr/ppermute | solution.py:13
  470.9 9.6 %collective-permute-start = (bf16[32,1024]{1,0:T(8,128)(2,1)}, bf16[32,1024]{1,0:T(8,128)(2,1)S(1)}, u32[]{:S(2)}, u32[]{:S(2)}) collective-permute-start(bf16[32,1024]{1,0:T(8,128)(2,1)} %get-tuple-element.299), channel_id=1, source_target_pairs={{32,0},{64,32},{96,64},{128,96},{160,128},{192,160},{224,192},{256... | collective-permute-start | bytes 196616 | tf_op jit(solution)/shard_map/while/body/eval_jaxpr/ppermute | solution.py:13
  505.7 123.2 %copy-start.3 = (f32[1,4,1024]{2,1,0:T(4,128)}, f32[1,4,1024]{2,1,0:T(4,128)S(1)}, u32[]{:S(2)}) copy-start(f32[1,4,1024]{2,1,0:T(4,128)S(1)} %broadcast_in_dim_reshape.3) | copy-start | bytes 49156
Sparse Core Ops, SparseCore 0:
  10.1 103.0 all-gather.3
where the time goes:
time: 638 us; the launch traced here: 636 us
  waiting for transfers between devices  268 us (42%)
  blocking collectives  251 us (39%)
  matrix products  29.3 us (5%)
  between operations  28.8 us (5%)
  starting transfers between devices  24.5 us (4%)
  other arithmetic  18.2 us (3%)
  local copies, waits for them, and re-layouts  15.9 us (2%)
    ppermute x19, waiting for transfers between devices, from_behind(): return lax.ppermute(block, axis, route)  179 us
    all_gather x19, blocking collectives, advance(): grad_full = lax.all_gather(grad_piece, 'mp', axis=1, tiled=True)  122 us
    psum x1, blocking collectives, body(): summed = lax.psum(score_table * score_scale, ('section', 'dp', 'mp'))  99.2 us
    all_gather x1, waiting for transfers between devices, body(): w_rows = lax.all_gather(weights[0], 'dp', axis=1, tiled=True)  87.9 us
    dot_general x4, matrix products, through(): lax.dot_general(grad_full, w_rows, (((1,), (1,)), ((), ())), preferred_el...  26.4 us
    ppermute x19, starting transfers between devices, from_behind(): return lax.ppermute(block, axis, route)  24.5 us
    all_gather x1, blocking collectives, body(): lax.all_gather(panels_here, 'dp', axis=0, tiled=True)  18.5 us
    dynamic_update_slice x19, other arithmetic, advance(): lax.dynamic_update_slice_in_dim(stored, jnp.where(active, grad_piece, pre...  18.2 us
  transfers between devices with their start and end apart: 20, of which 20 were waited for; matrix products, arithmetic and copies ran while one was open for 0% of the time, Pallas kernels for 0%

commit v1 on v0

--- a/solution.py
+++ b/solution.py
@@ -43,7 +43,12 @@
     length = LEN
     examples = inputs.shape[0] // length
     low_rank = proj_in.shape[2]
-    w_rows = lax.all_gather(weights[0], "dp", axis=1, tiled=True)
+    ring = [weights[0]]
+    for hop in range(7):
+        ring.append(lax.ppermute(ring[-1], "dp", [(dev, (dev + 1) % 8) for dev in range(8)]))
+    w_rows = jnp.roll(
+        jnp.concatenate(ring[::-1], axis=1), (lax.axis_index("dp") + 1) * ring[0].shape[1], axis=1
+    )
     step_count = examples + section_count - 1
     top_section = section_count - 1
 

time: 638 us -> 743 us (1.16)
  waiting for transfers between devices: 268 us -> 325 us
  local copies, waits for them, and re-layouts: 15.9 us -> 53.7 us
  starting transfers between devices: 24.5 us -> 40.9 us
  between operations: 28.8 us -> 15.9 us
    ppermute x0 -> x7, waiting for transfers between devices: none -> 146 us  [body(): lax.ppermute(ring[-1], 'dp', [(dev, (dev + 1) % 8) for dev in range(8)])]
    all_gather x1 -> x0, waiting for transfers between devices: 87.9 us -> none  [body(): w_rows = lax.all_gather(weights[0], 'dp', axis=1, tiled=True)]
    unnamed x9 -> x38, local copies, waits for them, and re-layouts: 0.7 us -> 29.6 us
    ppermute x0 -> x7, starting transfers between devices: none -> 16.4 us  [body(): lax.ppermute(ring[-1], 'dp', [(dev, (dev + 1) % 8) for dev in range(8)])]
    dynamic_slice x0 -> x1, local copies, waits for them, and re-layouts: none -> 7.73 us  [body(): jnp.roll(jnp.concatenate(ring[::-1], axis=1), (lax.axis_index('dp') + 1)...]
  transfers between devices with their start and end apart: 20 -> 26, of which waited for: 20 -> 26; matrix products, arithmetic and copies ran while one was open for 0% -> 0% of each run, Pallas kernels for 0% -> 0%
where the time goes in v1:
time: 743 us; the launch traced here: 740 us
  waiting for transfers between devices  325 us (44%)
  blocking collectives  256 us (34%)
  local copies, waits for them, and re-layouts  53.7 us (7%)
  starting transfers between devices  40.9 us (6%)
  matrix products  29.5 us (4%)
  other arithmetic  18.2 us (2%)
  between operations  15.9 us (2%)
    ppermute x19, waiting for transfers between devices, from_behind(): return lax.ppermute(block, axis, route)  180 us
    ppermute x7, waiting for transfers between devices, body(): lax.ppermute(ring[-1], 'dp', [(dev, (dev + 1) % 8) for dev in range(8)])  146 us
    all_gather x19, blocking collectives, advance(): grad_full = lax.all_gather(grad_piece, 'mp', axis=1, tiled=True)  129 us
    psum x1, blocking collectives, body(): summed = lax.psum(score_table * score_scale, ('section', 'dp', 'mp'))  98.5 us
    unnamed x38, local copies, waits for them, and re-layouts  29.6 us
    dot_general x4, matrix products, through(): lax.dot_general(grad_full, w_rows, (((1,), (1,)), ((), ())), preferred_el...  26.4 us
    ppermute x19, starting transfers between devices, from_behind(): return lax.ppermute(block, axis, route)  24.5 us
    all_gather x1, blocking collectives, body(): lax.all_gather(panels_here, 'dp', axis=0, tiled=True)  18.3 us
  transfers between devices with their start and end apart: 26, of which 26 were waited for; matrix products, arithmetic and copies ran while one was open for 0% of the time, Pallas kernels for 0%

profile of v1, /device:TPU:1, one launch (start us, length us, event | category | flops | bytes accessed | tf_op | source)
XLA Modules:
  0.0 740.5 jit_solution(1612153399826048279)
XLA Ops:
  5.6 29.7 %collective-permute-done.1 = bf16[1024,512]{1,0:T(8,128)(2,1)S(1)} collective-permute-done((bf16[1024,512]{1,0:T(8,128)(2,1)}, bf16[1024,512]{1,0:T(8,128)(2,1)S(1)}, u32[]{:S(2)}, u32[]{:S(2)}) %collective-permute-start.1) | collective-permute-done | bytes 1048608 | tf_op jit(solution)/shard_map/ppermute | solution.py:48
  37.3 24.6 %collective-permute-done.2 = bf16[1024,512]{1,0:T(8,128)(2,1)S(1)} collective-permute-done((bf16[1024,512]{1,0:T(8,128)(2,1)S(1)}, bf16[1024,512]{1,0:T(8,128)(2,1)S(1)}, u32[]{:S(2)}, u32[]{:S(2)}) %collective-permute-start.2) | collective-permute-done | bytes 1048608 | tf_op jit(solution)/shard_map/ppermute | solution.py:48
  63.8 23.7 %collective-permute-done.3 = bf16[1024,512]{1,0:T(8,128)(2,1)S(1)} collective-permute-done((bf16[1024,512]{1,0:T(8,128)(2,1)S(1)}, bf16[1024,512]{1,0:T(8,128)(2,1)S(1)}, u32[]{:S(2)}, u32[]{:S(2)}) %collective-permute-start.3) | collective-permute-done | bytes 1048608 | tf_op jit(solution)/shard_map/ppermute | solution.py:48
  90.4 22.8 %collective-permute-done.4 = bf16[1024,512]{1,0:T(8,128)(2,1)S(1)} collective-permute-done((bf16[1024,512]{1,0:T(8,128)(2,1)S(1)}, bf16[1024,512]{1,0:T(8,128)(2,1)S(1)}, u32[]{:S(2)}, u32[]{:S(2)}) %collective-permute-start.4) | collective-permute-done | bytes 1048608 | tf_op jit(solution)/shard_map/ppermute | solution.py:48
  116.0 21.8 %collective-permute-done.5 = bf16[1024,512]{1,0:T(8,128)(2,1)S(1)} collective-permute-done((bf16[1024,512]{1,0:T(8,128)(2,1)S(1)}, bf16[1024,512]{1,0:T(8,128)(2,1)S(1)}, u32[]{:S(2)}, u32[]{:S(2)}) %collective-permute-start.5) | collective-permute-done | bytes 1048608 | tf_op jit(solution)/shard_map/ppermute | solution.py:48
  140.8 21.0 %collective-permute-done.6 = bf16[1024,512]{1,0:T(8,128)(2,1)} collective-permute-done((bf16[1024,512]{1,0:T(8,128)(2,1)S(1)}, bf16[1024,512]{1,0:T(8,128)(2,1)}, u32[]{:S(2)}, u32[]{:S(2)}) %collective-permute-start.6) | collective-permute-done | bytes 1048608 | tf_op jit(solution)/shard_map/ppermute | solution.py:48
  211.1 7.7 %constant_dynamic-slice_fusion.1 = bf16[1024,4096]{1,0:T(8,128)(2,1)} fusion(bf16[1024,8192]{1,0:T(8,128)(2,1)} %constant_dynamic-update-slice_fusion, s32[]{:T(128)S(6)} %select_n.111), kind=kLoop, calls=%fused_computation.78 | loop fusion | bytes 16777220 | tf_op jit(solution)/shard_map/jit(_roll_dynamic)/dynamic_slice | solution.py:49
  219.4 387.3 %while.17 = (s32[]{:T(128)}, bf16[32,1024]{1,0:T(8,128)(2,1)}, bf16[128,1024]{1,0:T(8,128)(2,1)S(1)}, s32[]{:T(128)}, pred[]{:T(512)}, /*index=5*/bf16[128,1024]...) while((s32[]{:T(128)}, bf16[32,1024]{1,0:T(8,128)(2,1)}, ...), condition=%wide.region_4.5_spmd, body=%wide.region_1.4_spmd.sunk | while | flops 268959744 | bytes 9830719 | solution.py:90
  225.7 13.5 %all_gather.14 = bf16[32,4096]{1,0:T(8,128)(2,1)S(1)} all-gather(bf16[32,1024]{1,0:T(8,128)(2,1)S(1)} %get-tuple-element.282), channel_id=1, replica_groups=mesh['section'=16,'dp'=8,'mp'=4] {'mp'}, dimensions={1}, use_global_device_ids=true | all-gather | bytes 327680 | tf_op jit(solution)/shard_map/while/body/eval_jaxpr/all_gather | solution.py:67
  246.5 6.6 all_gather.14
  260.3 6.6 all_gather.14
  275.1 6.4 all_gather.14
  373.8 8.2 %collective-permute-done = bf16[32,1024]{1,0:T(8,128)(2,1)S(1)} collective-permute-done((bf16[32,1024]{1,0:T(8,128)(2,1)}, bf16[32,1024]{1,0:T(8,128)(2,1)S(1)}, u32[]{:S(2)}, u32[]{:S(2)}) %collective-permute-start) | collective-permute-done | bytes 65568 | tf_op jit(solution)/shard_map/while/body/eval_jaxpr/ppermute | solution.py:13
  391.3 8.2 %collective-permute-done = bf16[32,1024]{1,0:T(8,128)(2,1)S(1)} collective-permute-done((bf16[32,1024]{1,0:T(8,128)(2,1)}, bf16[32,1024]{1,0:T(8,128)(2,1)S(1)}, u32[]{:S(2)}, u32[]{:S(2)}) %collective-permute-start) | collective-permute-done | bytes 65568 | tf_op jit(solution)/shard_map/while/body/eval_jaxpr/ppermute | solution.py:13
  408.7 8.2 %collective-permute-done = bf16[32,1024]{1,0:T(8,128)(2,1)S(1)} collective-permute-done((bf16[32,1024]{1,0:T(8,128)(2,1)}, bf16[32,1024]{1,0:T(8,128)(2,1)S(1)}, u32[]{:S(2)}, u32[]{:S(2)}) %collective-permute-start) | collective-permute-done | bytes 65568 | tf_op jit(solution)/shard_map/while/body/eval_jaxpr/ppermute | solution.py:13
  426.1 8.2 %collective-permute-done = bf16[32,1024]{1,0:T(8,128)(2,1)S(1)} collective-permute-done((bf16[32,1024]{1,0:T(8,128)(2,1)}, bf16[32,1024]{1,0:T(8,128)(2,1)S(1)}, u32[]{:S(2)}, u32[]{:S(2)}) %collective-permute-start) | collective-permute-done | bytes 65568 | tf_op jit(solution)/shard_map/while/body/eval_jaxpr/ppermute | solution.py:13
  443.6 8.2 %collective-permute-done = bf16[32,1024]{1,0:T(8,128)(2,1)S(1)} collective-permute-done((bf16[32,1024]{1,0:T(8,128)(2,1)}, bf16[32,1024]{1,0:T(8,128)(2,1)S(1)}, u32[]{:S(2)}, u32[]{:S(2)}) %collective-permute-start) | collective-permute-done | bytes 65568 | tf_op jit(solution)/shard_map/while/body/eval_jaxpr/ppermute | solution.py:13
  461.0 61.5 %collective-permute-done = bf16[32,1024]{1,0:T(8,128)(2,1)S(1)} collective-permute-done((bf16[32,1024]{1,0:T(8,128)(2,1)}, bf16[32,1024]{1,0:T(8,128)(2,1)S(1)}, u32[]{:S(2)}, u32[]{:S(2)}) %collective-permute-start) | collective-permute-done | bytes 65568 | tf_op jit(solution)/shard_map/while/body/eval_jaxpr/ppermute | solution.py:13
  529.9 6.6 conditional.2
  529.9 6.6 fusion
  537.8 8.2 %collective-permute-done = bf16[32,1024]{1,0:T(8,128)(2,1)S(1)} collective-permute-done((bf16[32,1024]{1,0:T(8,128)(2,1)}, bf16[32,1024]{1,0:T(8,128)(2,1)S(1)}, u32[]{:S(2)}, u32[]{:S(2)}) %collective-permute-start) | collective-permute-done | bytes 65568 | tf_op jit(solution)/shard_map/while/body/eval_jaxpr/ppermute | solution.py:13
  553.3 6.6 conditional.2
  553.3 6.6 fusion
  561.2 8.2 %collective-permute-done = bf16[32,1024]{1,0:T(8,128)(2,1)S(1)} collective-permute-done((bf16[32,1024]{1,0:T(8,128)(2,1)}, bf16[32,1024]{1,0:T(8,128)(2,1)S(1)}, u32[]{:S(2)}, u32[]{:S(2)}) %collective-permute-start) | collective-permute-done | bytes 65568 | tf_op jit(solution)/shard_map/while/body/eval_jaxpr/ppermute | solution.py:13
  576.7 6.6 conditional.2
  576.7 6.6 fusion
  584.6 8.2 %collective-permute-done = bf16[32,1024]{1,0:T(8,128)(2,1)S(1)} collective-permute-done((bf16[32,1024]{1,0:T(8,128)(2,1)}, bf16[32,1024]{1,0:T(8,128)(2,1)S(1)}, u32[]{:S(2)}, u32[]{:S(2)}) %collective-permute-start) | collective-permute-done | bytes 65568 | tf_op jit(solution)/shard_map/while/body/eval_jaxpr/ppermute | solution.py:13
  600.1 6.6 conditional.2
  600.1 6.6 fusion
  607.1 10.8 %all-reduce = (bf16[4,32,64]{2,1,0:T(8,128)(2,1)S(1)}, bf16[128,64]{0,1:T(8,128)(2,1)S(1)}) all-reduce(bf16[4,32,64]{2,1,0:T(8,128)(2,1)S(1)} %bitcast.106, bf16[128,64]{0,1:T(8,128)(2,1)S(1)} %convolution_convert_fusion.1), channel_id=1, replica_groups=mesh['section'=16,'dp'=8,'mp'=4] {'mp'}, use_global_device_ids=true, to_apply=%region_5.6 | all-reduce | flops 16384 | bytes 65536 | tf_op jit(solution)/shard_map/psum | solution.py:97
  618.2 18.3 %all-gather = f32[8,4,1024]{2,1,0:T(4,128)S(1)} all-gather(f32[1,4,1024]{2,1,0:T(4,128)S(1)} %broadcast_in_dim_reshape.3), channel_id=1, replica_groups=mesh['section'=16,'dp'=8,'mp'=4] {'dp'}, dimensions={0}, use_global_device_ids=true | all-gather | bytes 147456 | tf_op jit(solution)/shard_map/all_gather | solution.py:113
  641.2 98.5 %psum.23 = f32[16,8,4]{1,0,2:T(8,128)S(1)} all-reduce(f32[16,8,4]{1,0,2:T(8,128)S(1)} %bitcast.107), channel_id=1, replica_groups=mesh['section'=16,'dp'=8,'mp'=4] {'section','dp','mp'}, use_global_device_ids=true, to_apply=%region_6.7 | all-reduce | flops 512 | bytes 4096 | tf_op jit(solution)/shard_map/psum | solution.py:120
  (176 shorter events, 268.1 us)
Async XLA Ops:
  0.6 179.8 %copy-start = (bf16[1,128,1024]{2,1,0:T(8,128)(2,1)S(1)}, bf16[1,128,1024]{2,1,0:T(8,128)(2,1)}, u32[]{:S(2)}) copy-start(bf16[1,128,1024]{2,1,0:T(8,128)(2,1)} %param.13) | copy-start | bytes 786436
  0.6 209.3 %copy-start.1 = (bf16[1,1024,512]{2,1,0:T(8,128)(2,1)S(1)}, bf16[1,1024,512]{2,1,0:T(8,128)(2,1)}, u32[]{:S(2)}) copy-start(bf16[1,1024,512]{2,1,0:T(8,128)(2,1)} %param.15) | copy-start | bytes 3145732
  0.7 34.7 %collective-permute-start.1 = (bf16[1024,512]{1,0:T(8,128)(2,1)}, bf16[1024,512]{1,0:T(8,128)(2,1)S(1)}, u32[]{:S(2)}, u32[]{:S(2)}) collective-permute-start(bf16[1024,512]{1,0:T(8,128)(2,1)} %bitcast.104), channel_id=1, source_target_pairs={{0,4},{4,8},{8,12},{12,16},{16,20},{20,24},{24,28},{28,0},{1,5},{5... | collective-permute-start | bytes 3145736 | tf_op jit(solution)/shard_map/ppermute | solution.py:48
  35.4 26.5 %collective-permute-start.2 = (bf16[1024,512]{1,0:T(8,128)(2,1)S(1)}, bf16[1024,512]{1,0:T(8,128)(2,1)S(1)}, u32[]{:S(2)}, u32[]{:S(2)}) collective-permute-start(bf16[1024,512]{1,0:T(8,128)(2,1)S(1)} %collective-permute-done.1), channel_id=1, source_target_pairs={{0,4},{4,8},{8,12},{12,16},{16,20},{20,24},{24,28},{28,0},{1,5},{5... | collective-permute-start | bytes 3145736 | tf_op jit(solution)/shard_map/ppermute | solution.py:48
  61.9 25.6 %collective-permute-start.3 = (bf16[1024,512]{1,0:T(8,128)(2,1)S(1)}, bf16[1024,512]{1,0:T(8,128)(2,1)S(1)}, u32[]{:S(2)}, u32[]{:S(2)}) collective-permute-start(bf16[1024,512]{1,0:T(8,128)(2,1)S(1)} %collective-permute-done.2), channel_id=1, source_target_pairs={{0,4},{4,8},{8,12},{12,16},{16,20},{20,24},{24,28},{28,0},{1,5},{5... | collective-permute-start | bytes 3145736 | tf_op jit(solution)/shard_map/ppermute | solution.py:48
  88.5 24.7 %collective-permute-start.4 = (bf16[1024,512]{1,0:T(8,128)(2,1)S(1)}, bf16[1024,512]{1,0:T(8,128)(2,1)S(1)}, u32[]{:S(2)}, u32[]{:S(2)}) collective-permute-start(bf16[1024,512]{1,0:T(8,128)(2,1)S(1)} %collective-permute-done.3), channel_id=1, source_target_pairs={{0,4},{4,8},{8,12},{12,16},{16,20},{20,24},{24,28},{28,0},{1,5},{5... | collective-permute-start | bytes 3145736 | tf_op jit(solution)/shard_map/ppermute | solution.py:48
  114.1 23.8 %collective-permute-start.5 = (bf16[1024,512]{1,0:T(8,128)(2,1)S(1)}, bf16[1024,512]{1,0:T(8,128)(2,1)S(1)}, u32[]{:S(2)}, u32[]{:S(2)}) collective-permute-start(bf16[1024,512]{1,0:T(8,128)(2,1)S(1)} %collective-permute-done.4), channel_id=1, source_target_pairs={{0,4},{4,8},{8,12},{12,16},{16,20},{20,24},{24,28},{28,0},{1,5},{5... | collective-permute-start | bytes 3145736 | tf_op jit(solution)/shard_map/ppermute | solution.py:48
  138.8 22.9 %collective-permute-start.6 = (bf16[1024,512]{1,0:T(8,128)(2,1)S(1)}, bf16[1024,512]{1,0:T(8,128)(2,1)}, u32[]{:S(2)}, u32[]{:S(2)}) collective-permute-start(bf16[1024,512]{1,0:T(8,128)(2,1)S(1)} %collective-permute-done.5), channel_id=1, source_target_pairs={{0,4},{4,8},{8,12},{12,16},{16,20},{20,24},{24,28},{28,0},{1,5},{5... | collective-permute-start | bytes 3145736 | tf_op jit(solution)/shard_map/ppermute | solution.py:48
  161.8 22.2 %collective-permute-start.7 = (bf16[1024,512]{1,0:T(8,128)(2,1)}, bf16[1024,512]{1,0:T(8,128)(2,1)}, u32[]{:S(2)}, u32[]{:S(2)}) collective-permute-start(bf16[1024,512]{1,0:T(8,128)(2,1)} %collective-permute-done.6), channel_id=1, source_target_pairs={{0,4},{4,8},{8,12},{12,16},{16,20},{20,24},{24,28},{28,0},{1,5},{5... | collective-permute-start | bytes 3145736 | tf_op jit(solution)/shard_map/ppermute | solution.py:48
  180.5 26.2 %copy-start.3 = (bf16[1024,512]{1,0:T(8,128)(2,1)S(1)}, bf16[1024,512]{1,0:T(8,128)(2,1)}, u32[]{:S(2)}) copy-start(bf16[1024,512]{1,0:T(8,128)(2,1)} %copy-done.2) | copy-start | bytes 3145732
  219.4 387.3 %copy-start.9 = (bf16[1,1024,64]{1,2,0:T(8,128)(2,1)S(1)}, bf16[1,1024,64]{1,2,0:T(8,128)(2,1)}, u32[]{:S(2)}) copy-start(bf16[1,1024,64]{1,2,0:T(8,128)(2,1)} %param.17) | copy-start | bytes 393220
  219.4 417.0 %copy-start.8 = (f32[1,2,1024]{2,1,0:T(2,128)S(1)}, f32[1,2,1024]{2,1,0:T(2,128)}, u32[]{:S(2)}) copy-start(f32[1,2,1024]{2,1,0:T(2,128)} %param.18) | copy-start | bytes 24580
  219.4 5.3 collective-permute-start
  239.9 5.6 collective-permute-start
  253.7 5.6 collective-permute-start
  267.6 6.6 collective-permute-start
  282.1 7.1 collective-permute-start
  297.1 7.1 collective-permute-start
  312.2 7.1 collective-permute-start
  327.2 7.1 collective-permute-start
  342.2 7.1 collective-permute-start
  357.3 7.3 collective-permute-start
  372.5 9.5 %collective-permute-start = (bf16[32,1024]{1,0:T(8,128)(2,1)}, bf16[32,1024]{1,0:T(8,128)(2,1)S(1)}, u32[]{:S(2)}, u32[]{:S(2)}) collective-permute-start(bf16[32,1024]{1,0:T(8,128)(2,1)} %get-tuple-element.299), channel_id=1, source_target_pairs={{32,0},{64,32},{96,64},{128,96},{160,128},{192,160},{224,192},{256... | collective-permute-start | bytes 196616 | tf_op jit(solution)/shard_map/while/body/eval_jaxpr/ppermute | solution.py:13
  390.0 9.5 %collective-permute-start = (bf16[32,1024]{1,0:T(8,128)(2,1)}, bf16[32,1024]{1,0:T(8,128)(2,1)S(1)}, u32[]{:S(2)}, u32[]{:S(2)}) collective-permute-start(bf16[32,1024]{1,0:T(8,128)(2,1)} %get-tuple-element.299), channel_id=1, source_target_pairs={{32,0},{64,32},{96,64},{128,96},{160,128},{192,160},{224,192},{256... | collective-permute-start | bytes 196616 | tf_op jit(solution)/shard_map/while/body/eval_jaxpr/ppermute | solution.py:13
  407.4 9.5 %collective-permute-start = (bf16[32,1024]{1,0:T(8,128)(2,1)}, bf16[32,1024]{1,0:T(8,128)(2,1)S(1)}, u32[]{:S(2)}, u32[]{:S(2)}) collective-permute-start(bf16[32,1024]{1,0:T(8,128)(2,1)} %get-tuple-element.299), channel_id=1, source_target_pairs={{32,0},{64,32},{96,64},{128,96},{160,128},{192,160},{224,192},{256... | collective-permute-start | bytes 196616 | tf_op jit(solution)/shard_map/while/body/eval_jaxpr/ppermute | solution.py:13
  424.8 9.5 %collective-permute-start = (bf16[32,1024]{1,0:T(8,128)(2,1)}, bf16[32,1024]{1,0:T(8,128)(2,1)S(1)}, u32[]{:S(2)}, u32[]{:S(2)}) collective-permute-start(bf16[32,1024]{1,0:T(8,128)(2,1)} %get-tuple-element.299), channel_id=1, source_target_pairs={{32,0},{64,32},{96,64},{128,96},{160,128},{192,160},{224,192},{256... | collective-permute-start | bytes 196616 | tf_op jit(solution)/shard_map/while/body/eval_jaxpr/ppermute | solution.py:13
  442.3 9.5 %collective-permute-start = (bf16[32,1024]{1,0:T(8,128)(2,1)}, bf16[32,1024]{1,0:T(8,128)(2,1)S(1)}, u32[]{:S(2)}, u32[]{:S(2)}) collective-permute-start(bf16[32,1024]{1,0:T(8,128)(2,1)} %get-tuple-element.299), channel_id=1, source_target_pairs={{32,0},{64,32},{96,64},{128,96},{160,128},{192,160},{224,192},{256... | collective-permute-start | bytes 196616 | tf_op jit(solution)/shard_map/while/body/eval_jaxpr/ppermute | solution.py:13
  459.7 62.8 %collective-permute-start = (bf16[32,1024]{1,0:T(8,128)(2,1)}, bf16[32,1024]{1,0:T(8,128)(2,1)S(1)}, u32[]{:S(2)}, u32[]{:S(2)}) collective-permute-start(bf16[32,1024]{1,0:T(8,128)(2,1)} %get-tuple-element.299), channel_id=1, source_target_pairs={{32,0},{64,32},{96,64},{128,96},{160,128},{192,160},{224,192},{256... | collective-permute-start | bytes 196616 | tf_op jit(solution)/shard_map/while/body/eval_jaxpr/ppermute | solution.py:13
  536.5 9.5 %collective-permute-start = (bf16[32,1024]{1,0:T(8,128)(2,1)}, bf16[32,1024]{1,0:T(8,128)(2,1)S(1)}, u32[]{:S(2)}, u32[]{:S(2)}) collective-permute-start(bf16[32,1024]{1,0:T(8,128)(2,1)} %get-tuple-element.299), channel_id=1, source_target_pairs={{32,0},{64,32},{96,64},{128,96},{160,128},{192,160},{224,192},{256... | collective-permute-start | bytes 196616 | tf_op jit(solution)/shard_map/while/body/eval_jaxpr/ppermute | solution.py:13
  559.9 9.5 %collective-permute-start = (bf16[32,1024]{1,0:T(8,128)(2,1)}, bf16[32,1024]{1,0:T(8,128)(2,1)S(1)}, u32[]{:S(2)}, u32[]{:S(2)}) collective-permute-start(bf16[32,1024]{1,0:T(8,128)(2,1)} %get-tuple-element.299), channel_id=1, source_target_pairs={{32,0},{64,32},{96,64},{128,96},{160,128},{192,160},{224,192},{256... | collective-permute-start | bytes 196616 | tf_op jit(solution)/shard_map/while/body/eval_jaxpr/ppermute | solution.py:13
  583.3 9.5 %collective-permute-start = (bf16[32,1024]{1,0:T(8,128)(2,1)}, bf16[32,1024]{1,0:T(8,128)(2,1)S(1)}, u32[]{:S(2)}, u32[]{:S(2)}) collective-permute-start(bf16[32,1024]{1,0:T(8,128)(2,1)} %get-tuple-element.299), channel_id=1, source_target_pairs={{32,0},{64,32},{96,64},{128,96},{160,128},{192,160},{224,192},{256... | collective-permute-start | bytes 196616 | tf_op jit(solution)/shard_map/while/body/eval_jaxpr/ppermute | solution.py:13
  618.2 122.3 %copy-start.10 = (f32[1,4,1024]{2,1,0:T(4,128)}, f32[1,4,1024]{2,1,0:T(4,128)S(1)}, u32[]{:S(2)}) copy-start(f32[1,4,1024]{2,1,0:T(4,128)S(1)} %broadcast_in_dim_reshape.3) | copy-start | bytes 49156
  (5 other events, 52.1 us)
